TPU v7x, 256 devices: a whole 4x4x8 slice. The times are simulated.
256 devices in a mesh: pair: 16 (over z, core), virt: 16 (over x, y).
Axes of the slice: x: 4, y: 4, z: 8, core: 2. Of those that a mesh axis runs over, the one named last changes fastest.
Arguments:
- amplitudes: float32 [64, 2048, 4096], P('virt', 'pair'), may hold values from -0.9 to 0.9
- integrals: float32 [64, 384, 4096], P('virt', 'pair'), may hold values from -0.09375 to 0.09375
- tile_flags: int32 [64], P('virt'), may hold values 0 or 1
- live_count: int32 [16], replicated, may hold values from 1 to 4, as said below
- pair_occ: int32 [2048, 2], P(('pair', 'virt')), may hold values from 0 to 199
- occ_energy: float32 [200], replicated, may hold values from -2.5 to -0.3
- ab_energy: float32 [384], replicated, may hold values from 0.6 to 3
Outputs:
- ladder: float32 [2048, 384], P(('pair', 'virt'))
- update: float32 [2048, 384], P(('pair', 'virt'))
Inputs may be any that keep to these rules, and one draw needn't show every extreme that they name: `live_count`: entry v is how many of the 4 slots of virt index v hold tile pairs: its slots below that number do, and the contents of the others are not to be used. At some index it is 4, and at the index half the axis away it is 1.
All inputs are finite; a program needn't handle non-finite values. No bound on the sum of `tile_flags` on one device may be relied on, other than what follows from the above.
Results may differ from a plain program's by a relative error of at most 0.0001.
Values sent between devices are 32-bit elements; how exact they have to be, the bound alone decides.
No kernel may reach another device: no remote copies, remote signals or barrier semaphores. Data moves between devices by JAX's collectives and lax.ppermute only.
A program may use at most 128 MiB of HBM per device.

v0:
```python
import jax
import jax.numpy as jnp
from jax import lax
from jax.sharding import PartitionSpec as P

TILE = 64


def symmetric_rows(rows, flag):
    shaped = rows.reshape(rows.shape[0], TILE, TILE)
    swapped = jnp.swapaxes(shaped, 1, 2).reshape(rows.shape)
    return rows + flag.astype(jnp.float32) * swapped


def tile_product(amp_tile, int_rows):
    return lax.dot_general(
        amp_tile,
        int_rows,
        (((1,), (1,)), ((), ())),
        precision=lax.Precision.HIGHEST,
        preferred_element_type=jnp.float32,
    )


def on_device(amplitudes, integrals, tile_flags, live_count, pair_occ, occ_energy, ab_energy):
    slots, pair_rows, _ = amplitudes.shape
    virt_index = lax.axis_index("virt")
    n_virt = lax.axis_size("virt")
    own_count = live_count[virt_index]
    running = None
    for slot in range(slots):
        sym_rows = symmetric_rows(integrals[slot], tile_flags[slot])
        gathered = lax.all_gather(sym_rows, "pair", axis=0, tiled=True)
        term = tile_product(amplitudes[slot], gathered)
        term = jnp.where(slot < own_count, term, jnp.zeros_like(term))
        running = term if running is None else running + term
    ab = running.shape[1]
    blocks = running.reshape(n_virt, pair_rows // n_virt, ab)
    received = lax.all_to_all(blocks, "virt", 0, 0, tiled=False)
    ladder = jnp.sum(received, axis=0)
    occ_range = jnp.arange(occ_energy.shape[0], dtype=jnp.int32)
    first_energy = jnp.sum(
        jnp.where(pair_occ[:, 0:1] == occ_range[None, :], occ_energy[None, :], 0.0), axis=1
    )
    second_energy = jnp.sum(
        jnp.where(pair_occ[:, 1:2] == occ_range[None, :], occ_energy[None, :], 0.0), axis=1
    )
    denominator = ab_energy[None, :] - first_energy[:, None] - second_energy[:, None]
    return (ladder, ladder / denominator)


def solution(mesh):
    return jax.shard_map(
        on_device,
        mesh=mesh,
        in_specs=(
            P("virt", "pair", None),
            P("virt", "pair", None),
            P("virt"),
            P(),
            P(("pair", "virt"), None),
            P(),
            P(),
        ),
        out_specs=(P(("pair", "virt"), None), P(("pair", "virt"), None)),
        check_vma=False,
    )
```

profile of v0, /device:TPU:1, one launch (start us, length us, event | category | flops | bytes accessed | tf_op | source)
XLA Modules:
  0.0 243.5 jit_solution(8998881442713806201)
XLA Ops:
  7.2 1.4 fusion.36
  11.1 2.4 slice_multiply_fusion
  13.5 0.3 mul.62
  14.4 0.3 mul.67
  15.0 1.0 mul.69
  16.0 1.3 mul.72
  17.6 1.0 mul.74
  18.7 1.3 mul.77
  20.5 2.4 bitcast_add_fusion
  23.0 0.7 all-gather.9.cloned.1.call-update
  23.7 0.7 all-gather.5.cloned.1.call-update
  24.6 0.3 all-gather.11.cloned.1.call-update
  25.0 0.6 dynamic_slice.3
  28.2 45.1 %all-gather.7.cloned.1.call-done = f32[384,4096]{1,0:T(8,128)} async-done(((f32[24,4096]{1,0:T(8,128)}), f32[384,4096]{1,0:T(8,128)}) %all-gather.7.cloned.1.call-update) | async-done | bytes 6291472 | tf_op jit(solution)/shard_map/all_gather | solution.py:33
  73.3 9.3 %fusion.21 = f32[384,128]{0,1:T(8,128)S(1)} fusion(f32[384,4096]{1,0:T(8,128)} %all-gather.7.cloned.1.call-done, f32[4,128,4096]{2,1,0:T(8,128)} %param.7, pred[]{:T(512)} %bitcast.5), kind=kOutput, calls=%fused_computation.15 | convolution fusion | flops 2415968256 | bytes 8585728 | tf_op jit(solution)/shard_map/dot_general | solution.py:16
  82.6 37.3 %all-gather.9.cloned.1.call-done = f32[384,4096]{1,0:T(8,128)} async-done(((f32[24,4096]{1,0:T(8,128)}), f32[384,4096]{1,0:T(8,128)}) %all-gather.9.cloned.1.call-update) | async-done | bytes 6291472 | tf_op jit(solution)/shard_map/all_gather | solution.py:33
  119.8 9.3 %fusion.24 = f32[384,128]{0,1:T(8,128)S(1)} fusion(f32[384,4096]{1,0:T(8,128)} %all-gather.9.cloned.1.call-done, f32[4,128,4096]{2,1,0:T(8,128)} %param.7, pred[]{:T(512)} %bitcast.10), kind=kOutput, calls=%fused_computation.16 | convolution fusion | flops 2415968256 | bytes 8585728 | tf_op jit(solution)/shard_map/dot_general | solution.py:16
  129.1 37.3 %all-gather.5.cloned.1.call-done = f32[384,4096]{1,0:T(8,128)} async-done(((f32[24,4096]{1,0:T(8,128)}), f32[384,4096]{1,0:T(8,128)}) %all-gather.5.cloned.1.call-update) | async-done | bytes 6291472 | tf_op jit(solution)/shard_map/all_gather | solution.py:33
  166.4 9.5 %fusion.18 = f32[384,128]{0,1:T(8,128)S(1)} fusion(f32[384,128]{0,1:T(8,128)S(1)} %fusion.24, f32[384,128]{0,1:T(8,128)S(1)} %fusion.21, f32[384,4096]{1,0:T(8,128)} %all-gather.5.cloned.1.call-done, f32[4,128,4096]{2,1,0:T(8,128)} %param.7, pred[]{:T(512)} %bitcast), kind=kOutput, calls=%fused_computation.14 | convolution fusion | flops 2416066560 | bytes 8978944 | tf_op jit(solution)/shard_map/dot_general | solution.py:16
  175.9 36.8 %all-gather.11.cloned.1.call-done = f32[384,4096]{1,0:T(8,128)} async-done(((f32[24,4096]{1,0:T(8,128)}), f32[384,4096]{1,0:T(8,128)}) %all-gather.11.cloned.1.call-update) | async-done | bytes 6291472 | tf_op jit(solution)/shard_map/all_gather | solution.py:33
  212.8 9.9 %fusion.33 = f32[16,8,384]{2,1,0:T(8,128)} fusion(f32[384,128]{0,1:T(8,128)S(1)} %fusion.18, f32[384,4096]{1,0:T(8,128)} %all-gather.11.cloned.1.call-done, f32[4,128,4096]{2,1,0:T(8,128)} %param.7, pred[]{:T(512)} %bitcast.15), kind=kOutput, calls=%fused_computation.19 | convolution fusion | flops 2416017408 | bytes 8782336 | tf_op jit(solution)/shard_map/dot_general | solution.py:16
  222.7 6.5 %all-to-all-start = ((f32[16,8,384]{2,1,0:T(8,128)}), f32[16,8,384]{2,1,0:T(8,128)S(1)}, u32[]{:S(2)}, u32[]{:S(2)}) async-start(f32[16,8,384]{2,1,0:T(8,128)} %fusion.33), calls=%async_computation | async-start | bytes 393216 | tf_op jit(solution)/shard_map/all_to_all | solution.py:39
  229.5 6.8 %all-to-all-done = f32[16,8,384]{2,1,0:T(8,128)S(1)} async-done(((f32[16,8,384]{2,1,0:T(8,128)}), f32[16,8,384]{2,1,0:T(8,128)S(1)}, u32[]{:S(2)}, u32[]{:S(2)}) %all-to-all-start) | async-done | bytes 196640 | tf_op jit(solution)/shard_map/all_to_all | solution.py:39
  236.3 0.7 subtract_divide_fusion
  (26 shorter events, 2.3 us)
Async XLA Ops:
  7.2 66.1 %all-gather.7.cloned.1.call-start = ((), (), s32[]{:S(2)}) async-start(), calls=%async_computation.2 | async-start | bytes 6684672 | tf_op jit(solution)/shard_map/all_gather | solution.py:33
  14.1 6.4 %copy-start = (f32[4,24,4096]{2,1,0:T(8,128)S(1)}, f32[4,24,4096]{2,1,0:T(8,128)}, u32[]{:S(2)}) copy-start(f32[4,24,4096]{2,1,0:T(8,128)} %param.8) | copy-start | bytes 4718596
  17.3 7.7 %copy-start.5 = (s32[16]{0:T(128)S(1)}, s32[16]{0:T(128)}, u32[]{:S(2)}) copy-start(s32[16]{0:T(128)} %param.10) | copy-start | bytes 196
  22.9 96.9 %all-gather.9.cloned.1.call-start = ((), (), s32[]{:S(2)}) async-start(), calls=%async_computation.3 | async-start | bytes 6684672 | tf_op jit(solution)/shard_map/all_gather | solution.py:33
  23.7 142.7 %all-gather.5.cloned.1.call-start = ((), (), s32[]{:S(2)}) async-start(), calls=%async_computation.1 | async-start | bytes 6684672 | tf_op jit(solution)/shard_map/all_gather | solution.py:33
  24.4 188.3 %all-gather.11.cloned.1.call-start = ((), (), s32[]{:S(2)}) async-start(), calls=%async_computation.4 | async-start | bytes 6684672 | tf_op jit(solution)/shard_map/all_gather | solution.py:33
  175.9 53.4 %copy-start.4 = (s32[8,2]{0,1:T(2,128)S(1)}, s32[8,2]{0,1:T(2,128)}, u32[]{:S(2)}) copy-start(s32[8,2]{0,1:T(2,128)} %param.11) | copy-start | bytes 196
  175.9 53.4 %copy-start.3 = (f32[200]{0:T(256)S(1)}, f32[200]{0:T(256)}, u32[]{:S(2)}) copy-start(f32[200]{0:T(256)} %param.12) | copy-start | bytes 2404
  175.9 60.4 %copy-start.2 = (f32[384]{0:T(512)S(1)}, f32[384]{0:T(512)}, u32[]{:S(2)}) copy-start(f32[384]{0:T(512)} %param.13) | copy-start | bytes 4612
  222.7 13.5 %all-to-all-start = ((f32[16,8,384]{2,1,0:T(8,128)}), f32[16,8,384]{2,1,0:T(8,128)S(1)}, u32[]{:S(2)}, u32[]{:S(2)}) async-start(f32[16,8,384]{2,1,0:T(8,128)} %fusion.33), calls=%async_computation | async-start | bytes 393216 | tf_op jit(solution)/shard_map/all_to_all | solution.py:39
  236.3 0.7 copy-start.1
Sparse Core Ops, SparseCore 0:
  23.0 50.2 all-gather.6
  75.1 44.6 all-gather.8
  121.7 44.6 all-gather.4
  168.1 44.6 all-gather.10
where the time goes:
time: 244 us; the launch traced here: 243 us
  waiting for transfers between devices  165 us (68%)
  matrix products  38 us (16%)
  between operations  19 us (8%)
  local copies, waits for them, and re-layouts  8.98 us (4%)
  starting transfers between devices  6.86 us (3%)
  other arithmetic  5.67 us (2%)
    all_gather x4, waiting for transfers between devices, on_device(): gathered = lax.all_gather(sym_rows, 'pair', axis=0, tiled=True)  157 us
    dot_general x4, matrix products, tile_product(): lax.dot_general(amp_tile, int_rows, (((1,), (1,)), ((), ())), precision=l...  38 us
    mul x12, local copies, waits for them, and re-layouts, symmetric_rows(): return rows + flag.astype(jnp.float32) * swapped  6.94 us
    all_to_all x1, waiting for transfers between devices, on_device(): received = lax.all_to_all(blocks, 'virt', 0, 0, tiled=False)  6.75 us
    all_to_all x1, starting transfers between devices, on_device(): received = lax.all_to_all(blocks, 'virt', 0, 0, tiled=False)  6.52 us
  transfers between devices with their start and end apart: 5, of which 5 were waited for; matrix products, arithmetic and copies ran while one was open for 12% of the time, Pallas kernels for 0%

commit v1 on v0

--- a/solution.py
+++ b/solution.py
@@ -4,6 +4,39 @@
 from jax.sharding import PartitionSpec as P
 
 TILE = 64
+
+
+def view_columns_on(array_dim, here_x):
+    part_next = lax.axis_size("pair")
+    local_next, u1, even = (part_next, lax.axis_index("pair"), here_x.shape[array_dim])
+    extra = side_arr = here_x
+    t_next = lax.dynamic_update_slice_in_dim(
+        jnp.zeros(
+            [w * local_next if at == array_dim else w for at, w in enumerate(here_x.shape)],
+            here_x.dtype,
+        ),
+        here_x,
+        u1 * even,
+        axis=array_dim,
+    )
+    for to_i in range(1, local_next // 2 + 1):
+        plain = range(local_next)
+        m_next = map(lambda at: (at, (at + 1) % local_next), plain)
+        a_next = list(m_next)
+        extra = lax.ppermute(extra, "pair", a_next)
+        t_next = lax.dynamic_update_slice_in_dim(
+            t_next, extra, (u1 - to_i) % local_next * even, axis=array_dim
+        )
+        if 2 * to_i < local_next:
+            side_arr = lax.ppermute(
+                side_arr,
+                "pair",
+                list(map(lambda at: (at, (at - 1) % local_next), range(local_next))),
+            )
+            t_next = lax.dynamic_update_slice_in_dim(
+                t_next, side_arr, (u1 + to_i) % local_next * even, axis=array_dim
+            )
+    return t_next
 
 
 def symmetric_rows(rows, flag):
@@ -30,7 +63,7 @@
     running = None
     for slot in range(slots):
         sym_rows = symmetric_rows(integrals[slot], tile_flags[slot])
-        gathered = lax.all_gather(sym_rows, "pair", axis=0, tiled=True)
+        gathered = view_columns_on(0, sym_rows)
         term = tile_product(amplitudes[slot], gathered)
         term = jnp.where(slot < own_count, term, jnp.zeros_like(term))
         running = term if running is None else running + term

time: 244 us -> 221 us (0.906)
  the two profiles are of different devices: /device:TPU:1 before, /device:TPU:2 now
where the time goes in v1:
time: 221 us
  starting transfers between devices  92.6 us (42%)
  local copies, waits for them, and re-layouts  71.2 us (32%)
  matrix products  32.6 us (15%)
  waiting for transfers between devices  11 us (5%)
  other arithmetic  7.1 us (3%)
  between operations  6.17 us (3%)
    ppermute x28, starting transfers between devices, view_columns_on(): lax.ppermute(side_arr, 'pair', list(map(lambda at: (at, (at - 1) % local_...  85 us
    dot_general x4, matrix products, tile_product(): lax.dot_general(amp_tile, int_rows, (((1,), (1,)), ((), ())), precision=l...  32.6 us
    dynamic_update_slice x32, local copies, waits for them, and re-layouts, view_columns_on(): lax.dynamic_update_slice_in_dim(t_next, extra, (u1 - to_i) % local_next *...  28.2 us
    dynamic_update_slice x28, local copies, waits for them, and re-layouts, view_columns_on(): lax.dynamic_update_slice_in_dim(t_next, side_arr, (u1 + to_i) % local_nex...  23.9 us
    another operation x4, local copies, waits for them, and re-layouts  13.6 us
    all_to_all x1, starting transfers between devices, on_device(): received = lax.all_to_all(blocks, 'virt', 0, 0, tiled=False)  7.48 us
    all_to_all x1, waiting for transfers between devices, on_device(): received = lax.all_to_all(blocks, 'virt', 0, 0, tiled=False)  6.34 us
    ppermute x32, waiting for transfers between devices, view_columns_on(): extra = lax.ppermute(extra, 'pair', a_next)  4.57 us
  transfers between devices with their start and end apart: 61, of which 3 were waited for; matrix products, arithmetic and copies ran while one was open for 42% of the time, Pallas kernels for 0%

profile of v1, /device:TPU:2, one launch (start us, length us, event | category | flops | bytes accessed | tf_op | source)
XLA Modules:
  0.0 220.6 jit_solution(18061038503843737480)
XLA Ops:
  8.0 3.4 %broadcast.62.clone = f32[384,4096]{1,0:T(8,128)} broadcast(f32[]{:T(128)} %constant.191.clone.1), dimensions={} | broadcast | bytes 6291460 | tf_op jit(solution)/shard_map/broadcast.3
  12.4 5.3 %collective-permute-start.46 = (f32[24,4096]{1,0:T(8,128)}, f32[24,4096]{1,0:T(8,128)}, u32[]{:S(2)}, u32[]{:S(2)}) collective-permute-start(f32[24,4096]{1,0:T(8,128)} %get-tuple-element.11), channel_id=1, source_target_pairs={{0,240},{16,0},{32,16},{48,32},{64,48},{80,64},{96,80},{112,96},{1... | collective-permute-start | bytes 1179656 | tf_op jit(solution)/shard_map/ppermute | solution.py:31
  18.6 3.5 %broadcast.62.clone.1 = f32[384,4096]{1,0:T(8,128)} broadcast(f32[]{:T(128)} %constant.191.clone.1), dimensions={} | broadcast | bytes 6291460 | tf_op jit(solution)/shard_map/broadcast.3
  23.0 3.0 %collective-permute-start.31 = (f32[24,4096]{1,0:T(8,128)}, f32[24,4096]{1,0:T(8,128)}, u32[]{:S(2)}, u32[]{:S(2)}) collective-permute-start(f32[24,4096]{1,0:T(8,128)} %get-tuple-element.9), channel_id=1, source_target_pairs={{0,240},{16,0},{32,16},{48,32},{64,48},{80,64},{96,80},{112,96},{1... | collective-permute-start | bytes 1179656 | tf_op jit(solution)/shard_map/ppermute | solution.py:31
  26.8 3.3 %broadcast.62.clone.2 = f32[384,4096]{1,0:T(8,128)} broadcast(f32[]{:T(128)} %constant.191.clone.1), dimensions={} | broadcast | bytes 6291460 | tf_op jit(solution)/shard_map/broadcast.3
  32.0 3.4 %broadcast.62.clone.3 = f32[384,4096]{1,0:T(8,128)} broadcast(f32[]{:T(128)} %constant.191.clone.1), dimensions={} | broadcast | bytes 6291460 | tf_op jit(solution)/shard_map/broadcast.3
  39.5 3.0 %collective-permute-start.16 = (f32[24,4096]{1,0:T(8,128)}, f32[24,4096]{1,0:T(8,128)S(1)}, u32[]{:S(2)}, u32[]{:S(2)}) collective-permute-start(f32[24,4096]{1,0:T(8,128)} %get-tuple-element.7), channel_id=1, source_target_pairs={{0,240},{16,0},{32,16},{48,32},{64,48},{80,64},{96,80},{112,96},{1... | collective-permute-start | bytes 1179656 | tf_op jit(solution)/shard_map/ppermute | solution.py:31
  46.1 3.0 %collective-permute-start.1 = (f32[24,4096]{1,0:T(8,128)S(1)}, f32[24,4096]{1,0:T(8,128)S(1)}, u32[]{:S(2)}, u32[]{:S(2)}) collective-permute-start(f32[24,4096]{1,0:T(8,128)S(1)} %get-tuple-element.5), channel_id=1, source_target_pairs={{0,240},{16,0},{32,16},{48,32},{64,48},{80,64},{96,80},{112,96},{1... | collective-permute-start | bytes 1179656 | tf_op jit(solution)/shard_map/ppermute | solution.py:31
  62.6 3.0 %collective-permute-start.18 = (f32[24,4096]{1,0:T(8,128)S(1)}, f32[24,4096]{1,0:T(8,128)S(1)}, u32[]{:S(2)}, u32[]{:S(2)}) collective-permute-start(f32[24,4096]{1,0:T(8,128)S(1)} %collective-permute-done.16), channel_id=1, source_target_pairs={{0,240},{16,0},{32,16},{48,32},{64,48},{80,64},{96,80},{112,96},{1... | collective-permute-start | bytes 1179656 | tf_op jit(solution)/shard_map/ppermute | solution.py:31
  85.3 2.9 %collective-permute-start.5 = (f32[24,4096]{1,0:T(8,128)S(1)}, f32[24,4096]{1,0:T(8,128)S(1)}, u32[]{:S(2)}, u32[]{:S(2)}) collective-permute-start(f32[24,4096]{1,0:T(8,128)S(1)} %collective-permute-done.3), channel_id=1, source_target_pairs={{0,240},{16,0},{32,16},{48,32},{64,48},{80,64},{96,80},{112,96},{1... | collective-permute-start | bytes 1179656 | tf_op jit(solution)/shard_map/ppermute | solution.py:31
  89.8 3.0 %collective-permute-start.52 = (f32[24,4096]{1,0:T(8,128)S(1)}, f32[24,4096]{1,0:T(8,128)S(1)}, u32[]{:S(2)}, u32[]{:S(2)}) collective-permute-start(f32[24,4096]{1,0:T(8,128)S(1)} %collective-permute-done.50), channel_id=1, source_target_pairs={{0,240},{16,0},{32,16},{48,32},{64,48},{80,64},{96,80},{112,96},{1... | collective-permute-start | bytes 1179656 | tf_op jit(solution)/shard_map/ppermute | solution.py:31
  94.3 3.0 %collective-permute-start.37 = (f32[24,4096]{1,0:T(8,128)S(1)}, f32[24,4096]{1,0:T(8,128)S(1)}, u32[]{:S(2)}, u32[]{:S(2)}) collective-permute-start(f32[24,4096]{1,0:T(8,128)S(1)} %collective-permute-done.35), channel_id=1, source_target_pairs={{0,240},{16,0},{32,16},{48,32},{64,48},{80,64},{96,80},{112,96},{1... | collective-permute-start | bytes 1179656 | tf_op jit(solution)/shard_map/ppermute | solution.py:31
  117.1 2.9 %collective-permute-start.24 = (f32[24,4096]{1,0:T(8,128)S(1)}, f32[24,4096]{1,0:T(8,128)S(1)}, u32[]{:S(2)}, u32[]{:S(2)}) collective-permute-start(f32[24,4096]{1,0:T(8,128)S(1)} %collective-permute-done.22), channel_id=1, source_target_pairs={{0,240},{16,0},{32,16},{48,32},{64,48},{80,64},{96,80},{112,96},{1... | collective-permute-start | bytes 1179656 | tf_op jit(solution)/shard_map/ppermute | solution.py:31
  126.1 3.0 %collective-permute-start.56 = (f32[24,4096]{1,0:T(8,128)S(1)}, f32[24,4096]{1,0:T(8,128)S(1)}, u32[]{:S(2)}, u32[]{:S(2)}) collective-permute-start(f32[24,4096]{1,0:T(8,128)S(1)} %collective-permute-done.54), channel_id=1, source_target_pairs={{0,240},{16,0},{32,16},{48,32},{64,48},{80,64},{96,80},{112,96},{1... | collective-permute-start | bytes 1179656 | tf_op jit(solution)/shard_map/ppermute | solution.py:31
  135.2 3.0 %collective-permute-start.26 = (f32[24,4096]{1,0:T(8,128)S(1)}, f32[24,4096]{1,0:T(8,128)S(1)}, u32[]{:S(2)}, u32[]{:S(2)}) collective-permute-start(f32[24,4096]{1,0:T(8,128)S(1)} %collective-permute-done.24), channel_id=1, source_target_pairs={{0,240},{16,0},{32,16},{48,32},{64,48},{80,64},{96,80},{112,96},{1... | collective-permute-start | bytes 1179656 | tf_op jit(solution)/shard_map/ppermute | solution.py:31
  139.7 3.0 %collective-permute-start.11 = (f32[24,4096]{1,0:T(8,128)S(1)}, f32[24,4096]{1,0:T(8,128)S(1)}, u32[]{:S(2)}, u32[]{:S(2)}) collective-permute-start(f32[24,4096]{1,0:T(8,128)S(1)} %collective-permute-done.9), channel_id=1, source_target_pairs={{0,240},{16,0},{32,16},{48,32},{64,48},{80,64},{96,80},{112,96},{1... | collective-permute-start | bytes 1179656 | tf_op jit(solution)/shard_map/ppermute | solution.py:31
  153.3 2.9 %collective-permute-start.28 = (f32[24,4096]{1,0:T(8,128)S(1)}, f32[24,4096]{1,0:T(8,128)S(1)}, u32[]{:S(2)}, u32[]{:S(2)}) collective-permute-start(f32[24,4096]{1,0:T(8,128)S(1)} %collective-permute-done.26), channel_id=1, source_target_pairs={{0,240},{16,0},{32,16},{48,32},{64,48},{80,64},{96,80},{112,96},{1... | collective-permute-start | bytes 1179656 | tf_op jit(solution)/shard_map/ppermute | solution.py:31
  157.8 3.0 %collective-permute-start.13 = (f32[24,4096]{1,0:T(8,128)S(1)}, f32[24,4096]{1,0:T(8,128)S(1)}, u32[]{:S(2)}, u32[]{:S(2)}) collective-permute-start(f32[24,4096]{1,0:T(8,128)S(1)} %collective-permute-done.11), channel_id=1, source_target_pairs={{0,240},{16,0},{32,16},{48,32},{64,48},{80,64},{96,80},{112,96},{1... | collective-permute-start | bytes 1179656 | tf_op jit(solution)/shard_map/ppermute | solution.py:31
  170.8 8.1 %fusion.27 = f32[384,128]{0,1:T(8,128)S(1)} fusion(f32[384,4096]{1,0:T(8,128)} %constant_dynamic-update-slice_fusion, f32[4,128,4096]{2,1,0:T(8,128)S(1)} %bitcast.65, pred[]{:T(512)} %bitcast.15), kind=kOutput, calls=%fused_computation.17 | convolution fusion | flops 2415968256 | bytes 8585217 | tf_op jit(solution)/shard_map/dot_general | solution.py:49
  179.7 7.9 %fusion.24 = f32[384,128]{0,1:T(8,128)S(1)} fusion(f32[384,4096]{1,0:T(8,128)} %constant_dynamic-update-slice_fusion.16, f32[4,128,4096]{2,1,0:T(8,128)S(1)} %bitcast.65, pred[]{:T(512)} %bitcast.10), kind=kOutput, calls=%fused_computation.16 | convolution fusion | flops 2415968256 | bytes 8585217 | tf_op jit(solution)/shard_map/dot_general | solution.py:49
  188.5 7.9 %fusion.21 = f32[384,128]{0,1:T(8,128)S(1)} fusion(f32[384,4096]{1,0:T(8,128)} %constant_dynamic-update-slice_fusion.32, f32[4,128,4096]{2,1,0:T(8,128)S(1)} %bitcast.65, pred[]{:T(512)} %bitcast.5), kind=kOutput, calls=%fused_computation.15 | convolution fusion | flops 2415968256 | bytes 8585217 | tf_op jit(solution)/shard_map/dot_general | solution.py:49
  197.2 8.6 %fusion.33 = f32[16,8,384]{2,1,0:T(8,128)} fusion(f32[384,128]{0,1:T(8,128)S(1)} %fusion.27, f32[384,128]{0,1:T(8,128)S(1)} %fusion.24, f32[384,128]{0,1:T(8,128)S(1)} %fusion.21, f32[384,4096]{1,0:T(8,128)} %constant_dynamic-update-slice_fusion.48, f32[4,128,4096]{2,1,0:T(8,128)S(1)} %bitcast.65, pred[]{:T(512)} %bitcast), kind=kOutput, calls=%fused_computation.19 | convolution fusion | flops 2416115712 | bytes 9175041 | tf_op jit(solution)/shard_map/dot_general | solution.py:49
  205.8 7.5 %all-to-all-start = ((f32[16,8,384]{2,1,0:T(8,128)}), f32[16,8,384]{2,1,0:T(8,128)S(1)}, u32[]{:S(2)}, u32[]{:S(2)}) async-start(f32[16,8,384]{2,1,0:T(8,128)} %fusion.33), calls=%async_computation | async-start | bytes 393216 | tf_op jit(solution)/shard_map/all_to_all | solution.py:72
  213.6 6.3 %all-to-all-done = f32[16,8,384]{2,1,0:T(8,128)S(1)} async-done(((f32[16,8,384]{2,1,0:T(8,128)}), f32[16,8,384]{2,1,0:T(8,128)S(1)}, u32[]{:S(2)}, u32[]{:S(2)}) %all-to-all-start) | async-done | bytes 196640 | tf_op jit(solution)/shard_map/all_to_all | solution.py:72
  (210 shorter events, 110.5 us)
Async XLA Ops:
  12.4 27.1 %collective-permute-start.45 = (f32[24,4096]{1,0:T(8,128)}, f32[24,4096]{1,0:T(8,128)}, u32[]{:S(2)}, u32[]{:S(2)}) collective-permute-start(f32[24,4096]{1,0:T(8,128)} %get-tuple-element.11), channel_id=1, source_target_pairs={{0,16},{16,32},{32,48},{48,64},{64,80},{80,96},{96,112},{112,128},... | collective-permute-start | bytes 1179656 | tf_op jit(solution)/shard_map/ppermute | solution.py:26
  12.4 33.7 %collective-permute-start.46 = (f32[24,4096]{1,0:T(8,128)}, f32[24,4096]{1,0:T(8,128)}, u32[]{:S(2)}, u32[]{:S(2)}) collective-permute-start(f32[24,4096]{1,0:T(8,128)} %get-tuple-element.11), channel_id=1, source_target_pairs={{0,240},{16,0},{32,16},{48,32},{64,48},{80,64},{96,80},{112,96},{1... | collective-permute-start | bytes 1179656 | tf_op jit(solution)/shard_map/ppermute | solution.py:31
  23.0 21.3 %collective-permute-start.30 = (f32[24,4096]{1,0:T(8,128)}, f32[24,4096]{1,0:T(8,128)}, u32[]{:S(2)}, u32[]{:S(2)}) collective-permute-start(f32[24,4096]{1,0:T(8,128)} %get-tuple-element.9), channel_id=1, source_target_pairs={{0,16},{16,32},{32,48},{48,64},{64,80},{80,96},{96,112},{112,128},... | collective-permute-start | bytes 1179656 | tf_op jit(solution)/shard_map/ppermute | solution.py:26
  23.0 27.9 %collective-permute-start.31 = (f32[24,4096]{1,0:T(8,128)}, f32[24,4096]{1,0:T(8,128)}, u32[]{:S(2)}, u32[]{:S(2)}) collective-permute-start(f32[24,4096]{1,0:T(8,128)} %get-tuple-element.9), channel_id=1, source_target_pairs={{0,240},{16,0},{32,16},{48,32},{64,48},{80,64},{96,80},{112,96},{1... | collective-permute-start | bytes 1179656 | tf_op jit(solution)/shard_map/ppermute | solution.py:31
  31.1 21.5 %collective-permute-start.15 = (f32[24,4096]{1,0:T(8,128)}, f32[24,4096]{1,0:T(8,128)}, u32[]{:S(2)}, u32[]{:S(2)}) collective-permute-start(f32[24,4096]{1,0:T(8,128)} %get-tuple-element.7), channel_id=1, source_target_pairs={{0,16},{16,32},{32,48},{48,64},{64,80},{80,96},{96,112},{112,128},... | collective-permute-start | bytes 1179656 | tf_op jit(solution)/shard_map/ppermute | solution.py:26
  39.5 17.8 %collective-permute-start.16 = (f32[24,4096]{1,0:T(8,128)}, f32[24,4096]{1,0:T(8,128)S(1)}, u32[]{:S(2)}, u32[]{:S(2)}) collective-permute-start(f32[24,4096]{1,0:T(8,128)} %get-tuple-element.7), channel_id=1, source_target_pairs={{0,240},{16,0},{32,16},{48,32},{64,48},{80,64},{96,80},{112,96},{1... | collective-permute-start | bytes 1179656 | tf_op jit(solution)/shard_map/ppermute | solution.py:31
  44.3 13.8 %collective-permute-start = (f32[24,4096]{1,0:T(8,128)S(1)}, f32[24,4096]{1,0:T(8,128)S(1)}, u32[]{:S(2)}, u32[]{:S(2)}) collective-permute-start(f32[24,4096]{1,0:T(8,128)S(1)} %get-tuple-element.5), channel_id=1, source_target_pairs={{0,16},{16,32},{32,48},{48,64},{64,80},{80,96},{96,112},{112,128},... | collective-permute-start | bytes 1179656 | tf_op jit(solution)/shard_map/ppermute | solution.py:26
  46.1 15.8 %collective-permute-start.1 = (f32[24,4096]{1,0:T(8,128)S(1)}, f32[24,4096]{1,0:T(8,128)S(1)}, u32[]{:S(2)}, u32[]{:S(2)}) collective-permute-start(f32[24,4096]{1,0:T(8,128)S(1)} %get-tuple-element.5), channel_id=1, source_target_pairs={{0,240},{16,0},{32,16},{48,32},{64,48},{80,64},{96,80},{112,96},{1... | collective-permute-start | bytes 1179656 | tf_op jit(solution)/shard_map/ppermute | solution.py:31
  52.6 14.6 %collective-permute-start.48 = (f32[24,4096]{1,0:T(8,128)}, f32[24,4096]{1,0:T(8,128)S(1)}, u32[]{:S(2)}, u32[]{:S(2)}) collective-permute-start(f32[24,4096]{1,0:T(8,128)} %collective-permute-done.46), channel_id=1, source_target_pairs={{0,240},{16,0},{32,16},{48,32},{64,48},{80,64},{96,80},{112,96},{1... | collective-permute-start | bytes 1179656 | tf_op jit(solution)/shard_map/ppermute | solution.py:31
  58.1 12.8 %collective-permute-start.33 = (f32[24,4096]{1,0:T(8,128)}, f32[24,4096]{1,0:T(8,128)S(1)}, u32[]{:S(2)}, u32[]{:S(2)}) collective-permute-start(f32[24,4096]{1,0:T(8,128)} %collective-permute-done.31), channel_id=1, source_target_pairs={{0,240},{16,0},{32,16},{48,32},{64,48},{80,64},{96,80},{112,96},{1... | collective-permute-start | bytes 1179656 | tf_op jit(solution)/shard_map/ppermute | solution.py:31
  62.6 12.8 %collective-permute-start.18 = (f32[24,4096]{1,0:T(8,128)S(1)}, f32[24,4096]{1,0:T(8,128)S(1)}, u32[]{:S(2)}, u32[]{:S(2)}) collective-permute-start(f32[24,4096]{1,0:T(8,128)S(1)} %collective-permute-done.16), channel_id=1, source_target_pairs={{0,240},{16,0},{32,16},{48,32},{64,48},{80,64},{96,80},{112,96},{1... | collective-permute-start | bytes 1179656 | tf_op jit(solution)/shard_map/ppermute | solution.py:31
  71.8 13.5 %collective-permute-start.50 = (f32[24,4096]{1,0:T(8,128)S(1)}, f32[24,4096]{1,0:T(8,128)S(1)}, u32[]{:S(2)}, u32[]{:S(2)}) collective-permute-start(f32[24,4096]{1,0:T(8,128)S(1)} %collective-permute-done.48), channel_id=1, source_target_pairs={{0,240},{16,0},{32,16},{48,32},{64,48},{80,64},{96,80},{112,96},{1... | collective-permute-start | bytes 1179656 | tf_op jit(solution)/shard_map/ppermute | solution.py:31
  85.3 12.8 %collective-permute-start.5 = (f32[24,4096]{1,0:T(8,128)S(1)}, f32[24,4096]{1,0:T(8,128)S(1)}, u32[]{:S(2)}, u32[]{:S(2)}) collective-permute-start(f32[24,4096]{1,0:T(8,128)S(1)} %collective-permute-done.3), channel_id=1, source_target_pairs={{0,240},{16,0},{32,16},{48,32},{64,48},{80,64},{96,80},{112,96},{1... | collective-permute-start | bytes 1179656 | tf_op jit(solution)/shard_map/ppermute | solution.py:31
  89.8 13.6 %collective-permute-start.52 = (f32[24,4096]{1,0:T(8,128)S(1)}, f32[24,4096]{1,0:T(8,128)S(1)}, u32[]{:S(2)}, u32[]{:S(2)}) collective-permute-start(f32[24,4096]{1,0:T(8,128)S(1)} %collective-permute-done.50), channel_id=1, source_target_pairs={{0,240},{16,0},{32,16},{48,32},{64,48},{80,64},{96,80},{112,96},{1... | collective-permute-start | bytes 1179656 | tf_op jit(solution)/shard_map/ppermute | solution.py:31
  94.3 12.9 %collective-permute-start.37 = (f32[24,4096]{1,0:T(8,128)S(1)}, f32[24,4096]{1,0:T(8,128)S(1)}, u32[]{:S(2)}, u32[]{:S(2)}) collective-permute-start(f32[24,4096]{1,0:T(8,128)S(1)} %collective-permute-done.35), channel_id=1, source_target_pairs={{0,240},{16,0},{32,16},{48,32},{64,48},{80,64},{96,80},{112,96},{1... | collective-permute-start | bytes 1179656 | tf_op jit(solution)/shard_map/ppermute | solution.py:31
  108.0 13.6 %collective-permute-start.54 = (f32[24,4096]{1,0:T(8,128)S(1)}, f32[24,4096]{1,0:T(8,128)S(1)}, u32[]{:S(2)}, u32[]{:S(2)}) collective-permute-start(f32[24,4096]{1,0:T(8,128)S(1)} %collective-permute-done.52), channel_id=1, source_target_pairs={{0,240},{16,0},{32,16},{48,32},{64,48},{80,64},{96,80},{112,96},{1... | collective-permute-start | bytes 1179656 | tf_op jit(solution)/shard_map/ppermute | solution.py:31
  117.1 12.8 %collective-permute-start.24 = (f32[24,4096]{1,0:T(8,128)S(1)}, f32[24,4096]{1,0:T(8,128)S(1)}, u32[]{:S(2)}, u32[]{:S(2)}) collective-permute-start(f32[24,4096]{1,0:T(8,128)S(1)} %collective-permute-done.22), channel_id=1, source_target_pairs={{0,240},{16,0},{32,16},{48,32},{64,48},{80,64},{96,80},{112,96},{1... | collective-permute-start | bytes 1179656 | tf_op jit(solution)/shard_map/ppermute | solution.py:31
  126.1 13.6 %collective-permute-start.56 = (f32[24,4096]{1,0:T(8,128)S(1)}, f32[24,4096]{1,0:T(8,128)S(1)}, u32[]{:S(2)}, u32[]{:S(2)}) collective-permute-start(f32[24,4096]{1,0:T(8,128)S(1)} %collective-permute-done.54), channel_id=1, source_target_pairs={{0,240},{16,0},{32,16},{48,32},{64,48},{80,64},{96,80},{112,96},{1... | collective-permute-start | bytes 1179656 | tf_op jit(solution)/shard_map/ppermute | solution.py:31
  144.3 13.6 %collective-permute-start.58 = (f32[24,4096]{1,0:T(8,128)S(1)}, f32[24,4096]{1,0:T(8,128)S(1)}, u32[]{:S(2)}, u32[]{:S(2)}) collective-permute-start(f32[24,4096]{1,0:T(8,128)S(1)} %collective-permute-done.56), channel_id=1, source_target_pairs={{0,240},{16,0},{32,16},{48,32},{64,48},{80,64},{96,80},{112,96},{1... | collective-permute-start | bytes 1179656 | tf_op jit(solution)/shard_map/ppermute | solution.py:31
  153.3 12.9 %collective-permute-start.28 = (f32[24,4096]{1,0:T(8,128)S(1)}, f32[24,4096]{1,0:T(8,128)S(1)}, u32[]{:S(2)}, u32[]{:S(2)}) collective-permute-start(f32[24,4096]{1,0:T(8,128)S(1)} %collective-permute-done.26), channel_id=1, source_target_pairs={{0,240},{16,0},{32,16},{48,32},{64,48},{80,64},{96,80},{112,96},{1... | collective-permute-start | bytes 1179656 | tf_op jit(solution)/shard_map/ppermute | solution.py:31
  162.4 16.6 %collective-permute-start.44 = (f32[24,4096]{1,0:T(8,128)S(1)}, f32[24,4096]{1,0:T(8,128)S(1)}, u32[]{:S(2)}, u32[]{:S(2)}) collective-permute-start(f32[24,4096]{1,0:T(8,128)S(1)} %collective-permute-done.42), channel_id=1, source_target_pairs={{0,16},{16,32},{32,48},{48,64},{64,80},{80,96},{96,112},{112,128},... | collective-permute-start | bytes 1179656 | tf_op jit(solution)/shard_map/ppermute | solution.py:26
  165.5 22.2 %collective-permute-start.29 = (f32[24,4096]{1,0:T(8,128)S(1)}, f32[24,4096]{1,0:T(8,128)S(1)}, u32[]{:S(2)}, u32[]{:S(2)}) collective-permute-start(f32[24,4096]{1,0:T(8,128)S(1)} %collective-permute-done.27), channel_id=1, source_target_pairs={{0,16},{16,32},{32,48},{48,64},{64,80},{80,96},{96,112},{112,128},... | collective-permute-start | bytes 1179656 | tf_op jit(solution)/shard_map/ppermute | solution.py:26
  166.2 30.2 %collective-permute-start.14 = (f32[24,4096]{1,0:T(8,128)S(1)}, f32[24,4096]{1,0:T(8,128)S(1)}, u32[]{:S(2)}, u32[]{:S(2)}) collective-permute-start(f32[24,4096]{1,0:T(8,128)S(1)} %collective-permute-done.12), channel_id=1, source_target_pairs={{0,16},{16,32},{32,48},{48,64},{64,80},{80,96},{96,112},{112,128},... | collective-permute-start | bytes 1179656 | tf_op jit(solution)/shard_map/ppermute | solution.py:26
  205.8 14.1 %all-to-all-start = ((f32[16,8,384]{2,1,0:T(8,128)}), f32[16,8,384]{2,1,0:T(8,128)S(1)}, u32[]{:S(2)}, u32[]{:S(2)}) async-start(f32[16,8,384]{2,1,0:T(8,128)} %fusion.33), calls=%async_computation | async-start | bytes 393216 | tf_op jit(solution)/shard_map/all_to_all | solution.py:72
  (47 other events, 536.9 us)
